TPU v7x, 128 devices: a whole 4x4x4 slice. The times are simulated.
128 devices in a mesh: req: 16 (over x, y), kv: 8 (over z, core).
Axes of the slice: x: 4, y: 4, z: 4, core: 2. Of those that a mesh axis runs over, the one named last changes fastest.
Arguments:
- hidden: bfloat16 [1024, 2048], P('req', 'kv'), may hold values from -6 to 6
- attn_gain: float32 [2048], replicated, may hold values from 0.25 to 1.75
- q_gain: float32 [128], replicated, may hold values from 0.25 to 1.75
- k_gain: float32 [128], replicated, may hold values from 0.25 to 1.75
- w_q: bfloat16 [2048, 2048], P(None, 'kv'), may hold values from -0.125 to 0.125
- w_gate_attn: bfloat16 [2048, 2048], P(None, 'kv'), may hold values from -0.125 to 0.125
- w_k: bfloat16 [2048, 1024], P(None, 'kv'), may hold values from -0.125 to 0.125
- w_v: bfloat16 [2048, 1024], P(None, 'kv'), may hold values from -0.125 to 0.125
- w_o: bfloat16 [2048, 2048], P('kv'), may hold values from -0.125 to 0.125
- k_pool: bfloat16 [2784, 128, 1024], P('req', None, 'kv'), may hold values from -245 to 245
- v_pool: bfloat16 [2784, 128, 1024], P('req', None, 'kv'), may hold values from -6 to 6
- lengths: int32 [1024], P('req'), may hold values from 1 to 4095, as said below
- page_table: int32 [1024, 32], P('req'), may hold values from 0 to 173, as said below
- mig_request: int32 [16, 16], P('req'), may hold values from 0 to 63, as said below
- mig_dest: int32 [16, 16], P('req'), may hold values from 0 to 15, as said below
- mlp_gain: float32 [2048], replicated, may hold values from 0.25 to 1.75
- w_gate: bfloat16 [2048, 6144], P(None, ('req', 'kv')), may hold values from -0.125 to 0.125
- w_up: bfloat16 [2048, 6144], P(None, ('req', 'kv')), may hold values from -0.125 to 0.125
- w_down: bfloat16 [2048, 6144], P(None, ('req', 'kv')), may hold values from -0.078125 to 0.078125
Outputs:
- out_hidden: bfloat16 [1024, 2048], P('req', 'kv')
- mig_keys: bfloat16 [256, 512, 1024], P('req', None, 'kv')
- mig_values: bfloat16 [256, 512, 1024], P('req', None, 'kv')
Inputs may be any that keep to these rules, and one draw needn't show every extreme that they name: lengths[r] tokens of request r are cached and its new token takes position lengths[r]; some request holds 4095 cached tokens. `page_table`: entries refer to the pool of the request's own device. The first lengths[r] // 128 + 1 entries of row r are the request's pages, distinct and never shared with another request of that device; later entries are valid pages that are not read. `mig_request`: row s names 16 different requests of device s; each has at most 511 cached tokens, and in every row one has exactly that many. `mig_dest`: each row is a permutation.
All inputs are finite; a program needn't handle non-finite values.
Results may differ from a plain program's by a relative error of at most 0.0093.
Values may be sent and summed in bfloat16 or wider, within the bound.
No kernel may reach another device: no remote copies, remote signals or barrier semaphores. Data moves between devices by JAX's collectives and lax.ppermute only.
A program may use at most 128 MiB of HBM per device.

v0:
```python
import jax
import jax.numpy as jnp
from jax import lax
from jax.sharding import PartitionSpec as P

MIGP = 4
EPSILON = 1e-06
ROPE_BASE = 1000000.0


def rms_norm(values, scale_row):
    values = values.astype(jnp.float32)
    return (
        values * lax.rsqrt(jnp.mean(values * values, axis=-1, keepdims=True) + EPSILON) * scale_row
    )


def rotate(values, position):
    half_dim = values.shape[-1] // 2
    frequency = ROPE_BASE ** (-jnp.arange(half_dim, dtype=jnp.float32) * 2.0 / values.shape[-1])
    angles = position.astype(jnp.float32)[:, None, None] * frequency
    cosine = jnp.cos(angles)
    sine_part = jnp.sin(angles)
    first_half = values[..., :half_dim]
    second = values[..., half_dim:]
    return jnp.concatenate(
        [first_half * cosine - second * sine_part, second * cosine + first_half * sine_part],
        axis=-1,
    )


def attend_pool(queries, new_keys, new_values, k_pool, v_pool, lengths, page_table):
    req_count, kv_local, group_size, head_dim = queries.shape
    pool_pages, page_size, _ = k_pool.shape
    table_width = page_table.shape[1]
    token_count = pool_pages * page_size
    score_scale = head_dim ** (-0.5)
    slot_ids = jnp.arange(table_width, dtype=jnp.int32)
    in_use = slot_ids[None, :] < (lengths // page_size + 1)[:, None]
    targets = jnp.where(in_use, page_table, pool_pages).reshape(-1)
    owner = (
        jnp.full((pool_pages,), -1, jnp.int32)
        .at[targets]
        .set(jnp.repeat(jnp.arange(req_count, dtype=jnp.int32), table_width), mode="drop")
    )
    first_pos = (
        jnp.zeros((pool_pages,), jnp.int32)
        .at[targets]
        .set(jnp.tile(slot_ids * page_size, req_count), mode="drop")
    )
    token_owner = jnp.repeat(owner, page_size)
    token_pos = (first_pos[:, None] + jnp.arange(page_size, dtype=jnp.int32)[None, :]).reshape(-1)
    valid = (token_owner[None, :] == jnp.arange(req_count, dtype=jnp.int32)[:, None]) & (
        token_pos[None, :] < lengths[:, None]
    )
    keys = k_pool.reshape(token_count, kv_local, head_dim)
    values = v_pool.reshape(token_count, kv_local, head_dim)
    scores = (
        jnp.einsum("rkgd,tkd->rkgt", queries, keys, preferred_element_type=jnp.float32)
        * score_scale
    )
    scores = jnp.where(valid[:, None, None, :], scores, -jnp.inf)
    own_score = (
        jnp.einsum("rkgd,rkd->rkg", queries, new_keys, preferred_element_type=jnp.float32)
        * score_scale
    )
    row_top = jnp.maximum(jnp.max(scores, axis=-1), own_score)
    exps_all = jnp.exp(scores - row_top[..., None])
    own_exp = jnp.exp(own_score - row_top)
    denom_sum = jnp.sum(exps_all, axis=-1) + own_exp
    weights = (exps_all / denom_sum[..., None]).astype(jnp.bfloat16)
    own_weight = (own_exp / denom_sum).astype(jnp.bfloat16)
    start_sum = jnp.einsum(
        "rkg,rkd->rkgd", own_weight, new_values, preferred_element_type=jnp.float32
    )
    return start_sum + jnp.einsum(
        "rkgt,tkd->rkgd", weights, values, preferred_element_type=jnp.float32
    )


def reduce_to_slice(partial, kv_count, slice_width):
    rows = partial.shape[0]
    pieces = partial.reshape(rows, kv_count, slice_width).transpose(1, 0, 2)
    arrived = lax.all_to_all(pieces, "kv", 0, 0, tiled=True)
    return jnp.sum(arrived, axis=0)


def per_device(
    hidden,
    attn_gain,
    q_gain,
    k_gain,
    w_q,
    w_gate_attn,
    w_k,
    w_v,
    w_o,
    k_pool,
    v_pool,
    lengths,
    page_table,
    mig_request,
    mig_dest,
    mlp_gain,
    w_gate,
    w_up,
    w_down,
):
    head_dim = q_gain.shape[0]
    req_count = hidden.shape[0]
    kv_local = w_k.shape[1] // head_dim
    q_local = w_q.shape[1] // head_dim
    group_size = q_local // kv_local
    page_size = k_pool.shape[1]
    channels = kv_local * head_dim
    model_width = mlp_gain.shape[0]
    gate_w = lax.all_gather(w_gate, "req", axis=1, tiled=True)
    up_w = lax.all_gather(w_up, "req", axis=1, tiled=True)
    down_w = lax.all_gather(w_down, "req", axis=1, tiled=True)
    whole_rows = lax.all_gather(hidden, "kv", axis=1, tiled=True)
    normed = rms_norm(whole_rows, attn_gain).astype(jnp.bfloat16)
    query_raw = jnp.dot(normed, w_q, preferred_element_type=jnp.float32).reshape(
        req_count, q_local, head_dim
    )
    gate_raw = jnp.dot(normed, w_gate_attn, preferred_element_type=jnp.float32)
    key_raw = jnp.dot(normed, w_k, preferred_element_type=jnp.float32).reshape(
        req_count, kv_local, head_dim
    )
    value_raw = jnp.dot(normed, w_v, preferred_element_type=jnp.float32).reshape(
        req_count, kv_local, head_dim
    )
    queries = rotate(rms_norm(query_raw, q_gain), lengths).astype(jnp.bfloat16)
    queries = queries.reshape(req_count, kv_local, group_size, head_dim)
    new_keys = rotate(rms_norm(key_raw, k_gain), lengths).astype(jnp.bfloat16)
    new_values = value_raw.astype(jnp.bfloat16)
    mig_rows = mig_request[0]
    dest_row = mig_dest[0]
    mig_count = mig_rows.shape[0]
    slot_count = MIGP * page_size
    moved_pages = page_table[mig_rows, :MIGP]
    slot_pos = jnp.arange(slot_count, dtype=jnp.int32)[None, :, None]
    moved_len = lengths[mig_rows][:, None, None]
    zero_value = jnp.zeros((), jnp.bfloat16)
    inverse = jnp.zeros_like(dest_row).at[dest_row].set(jnp.arange(mig_count, dtype=jnp.int32))

    def place_cache(pool, fresh_rows):
        cached = pool[moved_pages].reshape(mig_count, slot_count, channels)
        fresh_row = fresh_rows.reshape(req_count, channels)[mig_rows][:, None, :]
        filled = jnp.where(
            slot_pos < moved_len, cached, jnp.where(slot_pos == moved_len, fresh_row, zero_value)
        )
        return filled[inverse]

    mig_keys, mig_values = (
        lax.all_to_all(
            place_cache(k_pool, new_keys), "req", split_axis=0, concat_axis=0, tiled=True
        ),
        lax.all_to_all(
            place_cache(v_pool, new_values), "req", split_axis=0, concat_axis=0, tiled=True
        ),
    )
    context = attend_pool(queries, new_keys, new_values, k_pool, v_pool, lengths, page_table)
    gated = (jax.nn.sigmoid(gate_raw) * context.reshape(req_count, q_local * head_dim)).astype(
        jnp.bfloat16
    )
    head_terms = jnp.dot(gated, w_o, preferred_element_type=jnp.float32)
    kv_count = lax.axis_size("kv")
    slice_width = model_width // kv_count
    mid_slice = (
        hidden.astype(jnp.float32) + reduce_to_slice(head_terms, kv_count, slice_width)
    ).astype(jnp.bfloat16)
    mid_stream = lax.all_gather(mid_slice, "kv", axis=1, tiled=True)
    normed_mlp = rms_norm(mid_stream, mlp_gain).astype(jnp.bfloat16)
    gate_part = jnp.dot(normed_mlp, gate_w, preferred_element_type=jnp.float32)
    up_part = jnp.dot(normed_mlp, up_w, preferred_element_type=jnp.float32)
    activation = (jax.nn.silu(gate_part) * up_part).astype(jnp.bfloat16)
    down_part = jnp.einsum("ru,cu->rc", activation, down_w, preferred_element_type=jnp.float32)
    mlp_part = reduce_to_slice(down_part, kv_count, slice_width)
    out_hidden = (mid_slice.astype(jnp.float32) + mlp_part).astype(jnp.bfloat16)
    return (out_hidden, mig_keys, mig_values)


def solution(mesh):
    return jax.shard_map(
        per_device,
        mesh=mesh,
        in_specs=(
            P("req", "kv"),
            P(),
            P(),
            P(),
            P(None, "kv"),
            P(None, "kv"),
            P(None, "kv"),
            P(None, "kv"),
            P("kv", None),
            P("req", None, "kv"),
            P("req", None, "kv"),
            P("req"),
            P("req", None),
            P("req", None),
            P("req", None),
            P(),
            P(None, ("req", "kv")),
            P(None, ("req", "kv")),
            P(None, ("req", "kv")),
        ),
        out_specs=(P("req", "kv"), P("req", None, "kv"), P("req", None, "kv")),
        check_vma=False,
    )
```

profile of v0, /device:TPU:1, one launch (start us, length us, event | category | flops | bytes accessed | tf_op | source)
XLA Modules:
  0.0 233.5 jit_solution(11153392332926695177)
XLA Ops:
  8.7 15.6 %all_gather.15 = bf16[64,2048]{1,0:T(8,128)(2,1)S(1)} all-gather(bf16[64,256]{1,0:T(8,128)(2,1)} %param.19), channel_id=1, replica_groups=mesh['req'=16,'kv'=8] {'kv'}, dimensions={1}, use_global_device_ids=true | all-gather | bytes 294912 | tf_op jit(solution)/shard_map/all_gather | solution.py:120
  24.5 1.6 fusion.71
  28.9 8.0 %scatter_custom_fusion.1 = s32[174]{0:T(256)S(1)} fusion(s32[2048]{0:T(1024)S(1)} %bitcast.141, s32[2048]{0:T(1024)S(1)} %reshape.579, s32[]{:T(128)} %constant.29.clone.1), kind=kCustom, calls=%fused_computation.124 | custom fusion | bytes 700 | tf_op jit(solution)/shard_map/scatter | solution.py:49
  37.0 8.0 %scatter_custom_fusion = s32[174]{0:T(256)S(1)} fusion(s32[2048]{0:T(1024)S(1)} %bitcast.142, s32[2048]{0:T(1024)S(1)} %reshape.571, s32[]{:T(128)} %constant.27.clone.1), kind=kCustom, calls=%fused_computation.127 | custom fusion | bytes 700 | tf_op jit(solution)/shard_map/scatter | solution.py:44
  47.4 4.3 %fusion.75 = (f32[64,2]{0,1:T(2,128)S(1)}, f32[64,1,2,22272]{3,0,2,1:T(8,128)S(1)}) fusion(bf16[64,2,128]{2,0,1:T(8,128)(2,1)S(1)} %pad_maximum_fusion, bf16[22272,128,1]{1,0,2:T(8,128)(2,1)} %bitcast.133, pred[64,22272]{1,0:T(8,128)(4,1)S(1)} %fusion.5), kind=kOutput, calls=%fused_computation.141 | convolution fusion | flops 738361216 | bytes 18563584 | tf_op jit(solution)/shard_map/rkgd,tkd->rkgt/dot_general | solution.py:59
  51.8 2.3 fusion.2
  54.4 5.4 %fusion.15 = f32[64,1,2,128]{3,0,2,1:T(8,128)S(1)} fusion(bf16[22272,128,1]{1,0,2:T(8,128)(2,1)} %bitcast.139, f32[64,2]{0,1:T(2,128)S(1)} %get-tuple-element.12, f32[64,1,2,22272]{3,0,2,1:T(8,128)S(1)} %get-tuple-element.26, f32[64,2]{0,1:T(2,128)S(1)} %fusion.54, f32[64,128]{1,0:T(8,128)S(1)} %get-tuple-element.27, f32[64,2]{0,1:T(2,128)S(1)} %get-tuple-element.11), kind=kOutput, calls=%fused_computation.35 | convolution fusion | flops 738394112 | bytes 17204736 | tf_op jit(solution)/shard_map/rkgt,tkd->rkgd/dot_general | solution.py:76
  59.8 2.1 fusion.19
  62.7 4.3 %all-to-all-start = ((f32[8,64,256]{2,1,0:T(8,128)}), f32[8,64,256]{2,1,0:T(8,128)}, u32[]{:S(2)}, u32[]{:S(2)}) async-start(f32[8,64,256]{2,1,0:T(8,128)} %bitcast.131), calls=%async_computation | async-start | bytes 1048576 | tf_op jit(solution)/shard_map/all_to_all | solution.py:84
  70.8 3.7 %gather_fusion.4 = bf16[64,128,128]{2,1,0:T(8,128)(2,1)S(1)} fusion(bf16[174,128,128]{2,1,0:T(8,128)(2,1)} %param.29, s32[1024]{0:T(1024)S(1)} %pad_clamp_fusion.1), kind=kCustom, calls=%fused_computation.4 | custom fusion | bytes 4194560 | tf_op jit(solution)/shard_map/gather | solution.py:147
  74.5 4.8 %gather_fusion.1 = bf16[64,128,128]{2,1,0:T(8,128)(2,1)} fusion(bf16[174,128,128]{2,1,0:T(8,128)(2,1)} %param.28, s32[1024]{0:T(1024)S(1)} %pad_clamp_fusion.1), kind=kCustom, calls=%fused_computation.1 | custom fusion | bytes 4194560 | tf_op jit(solution)/shard_map/gather | solution.py:147
  82.0 7.2 %bitcast_select_fusion = (bf16[16,512,128]{2,1,0:T(8,128)(2,1)}, bf16[16,512,128]{2,1,0:T(8,128)(2,1)}) fusion(pred[16,512]{1,0:T(8,128)(4,1)S(1)} %get-tuple-element.18, pred[16,512]{1,0:T(8,128)(4,1)S(1)} %get-tuple-element.17, bf16[16,128]{1,0:T(8,128)(2,1)S(1)} %gather_fusion.5, bf16[16,128]{1,0:T(8,128)(2,1)S(1)} %gather_fusion.2, ...), kind=kLoop, calls=%fused_computation.24 | loop fusion | flops 4194304 | bytes 8413184 | tf_op jit(solution)/shard_map/jit(_where)/select_n | solution.py:149
  89.2 3.9 %gather_fusion.3 = bf16[16,512,128]{2,1,0:T(8,128)(2,1)} fusion(bf16[16,512,128]{2,1,0:T(8,128)(2,1)} %get-tuple-element.10, s32[1024]{0:T(1024)S(1)} %pad_clamp_fusion), kind=kCustom, calls=%fused_computation.3 | custom fusion | bytes 4194368 | tf_op jit(solution)/shard_map/gather | solution.py:152
  93.0 7.0 %all-to-all-start.2 = ((bf16[16,512,128]{2,1,0:T(8,128)(2,1)}), bf16[16,512,128]{2,1,0:T(8,128)(2,1)}, u32[]{:S(2)}, u32[]{:S(2)}) async-start(bf16[16,512,128]{2,1,0:T(8,128)(2,1)} %gather_fusion.3), calls=%async_computation.2 | async-start | bytes 4194304 | tf_op jit(solution)/shard_map/all_to_all | solution.py:155
  100.0 2.1 gather_fusion.6
  102.2 32.1 %all-to-all-done.2 = bf16[16,512,128]{2,1,0:T(8,128)(2,1)} async-done(((bf16[16,512,128]{2,1,0:T(8,128)(2,1)}), bf16[16,512,128]{2,1,0:T(8,128)(2,1)}, u32[]{:S(2)}, u32[]{:S(2)}) %all-to-all-start.2) | async-done | bytes 2097184 | tf_op jit(solution)/shard_map/all_to_all | solution.py:155
  134.3 7.8 %all-to-all-start.3 = ((bf16[16,512,128]{2,1,0:T(8,128)(2,1)}), bf16[16,512,128]{2,1,0:T(8,128)(2,1)S(1)}, u32[]{:S(2)}, u32[]{:S(2)}) async-start(bf16[16,512,128]{2,1,0:T(8,128)(2,1)} %gather_fusion.6), calls=%async_computation.3 | async-start | bytes 4194304 | tf_op jit(solution)/shard_map/all_to_all | solution.py:158
  143.2 14.0 %all_gather.16 = bf16[64,2048]{1,0:T(8,128)(2,1)S(1)} all-gather(bf16[64,256]{1,0:T(8,128)(2,1)S(1)} %add_convert_fusion.1), channel_id=1, replica_groups=mesh['req'=16,'kv'=8] {'kv'}, dimensions={1}, use_global_device_ids=true | all-gather | bytes 294912 | tf_op jit(solution)/shard_map/all_gather | solution.py:172
  157.4 3.7 %fusion.34 = f32[64,768]{1,0:T(8,128)} fusion(bf16[2048,768]{0,1:T(8,128)(2,1)} %all-gather.4.cloned.1.call-done, bf16[64,2048]{1,0:T(8,128)(2,1)S(1)} %all_gather.16, f32[2048]{0:T(1024)S(1)} %copy-done.7, f32[64]{0:T(128)S(1)} %add_rsqrt_fusion.1), kind=kOutput, calls=%fused_computation.58 | convolution fusion | flops 201850880 | bytes 3612928 | tf_op jit(solution)/shard_map/dot_general | solution.py:174
  161.0 36.9 %all-gather.8.cloned.1.call-done = bf16[2048,768]{0,1:T(8,128)(2,1)} async-done(((bf16[2048,48]{0,1:T(8,128)(2,1)}), bf16[2048,768]{0,1:T(8,128)(2,1)}) %all-gather.8.cloned.1.call-update) | async-done | bytes 3145744 | tf_op jit(solution)/shard_map/all_gather | solution.py:119
  197.9 5.9 %fusion.7 = f32[64,2048]{1,0:T(8,128)} fusion(bf16[2048,768]{0,1:T(8,128)(2,1)} %all-gather.8.cloned.1.call-done, bf16[2048,768]{0,1:T(8,128)(2,1)} %all-gather.6.cloned.1.call-done, f32[64,768]{1,0:T(8,128)} %fusion.34, bf16[64,2048]{1,0:T(8,128)(2,1)S(1)} %all_gather.16, f32[2048]{0:T(1024)S(1)} %copy-done.7, f32[64]{0:T(128)S(1)} %add_rsqrt_fusion.1), kind=kOutput, calls=%fused_computation.28 | convolution fusion | flops 403472384 | bytes 7282944 | tf_op jit(solution)/shard_map/ru,cu->rc/dot_general | solution.py:177
  203.8 1.9 copy.60
  205.7 15.1 %all_to_all.20 = f32[8,64,256]{2,1,0:T(8,128)} all-to-all(f32[8,64,256]{2,1,0:T(8,128)} %bitcast.138), channel_id=1, replica_groups=mesh['req'=16,'kv'=8] {'kv'}, dimensions={0} | all-to-all | bytes 1048576 | tf_op jit(solution)/shard_map/all_to_all | solution.py:84
  222.5 3.1 %copy.64 = bf16[16,512,128]{2,1,0:T(8,128)(2,1)} copy(bf16[16,512,128]{2,1,0:T(8,128)(2,1)} %all-to-all-done.2) | data formatting | bytes 4194304
  (102 shorter events, 18.6 us)
Async XLA Ops:
  7.2 52.6 %copy-start = (bf16[256,2048]{1,0:T(8,128)(2,1)S(1)}, bf16[256,2048]{1,0:T(8,128)(2,1)}, u32[]{:S(2)}) copy-start(bf16[256,2048]{1,0:T(8,128)(2,1)} %param.27) | copy-start | bytes 3145732
  7.2 37.9 %copy-start.1 = (s32[64]{0:T(128)S(1)}, s32[64]{0:T(128)}, u32[]{:S(2)}) copy-start(s32[64]{0:T(128)} %param.30) | copy-start | bytes 772
  7.2 21.4 %copy-start.2 = (s32[64,32]{0,1:T(8,128)S(1)}, s32[64,32]{0,1:T(8,128)}, u32[]{:S(2)}) copy-start(s32[64,32]{0,1:T(8,128)} %param.31) | copy-start | bytes 24580
  7.2 39.1 %copy-start.8 = (f32[128]{0:T(128)S(1)}, f32[128]{0:T(128)}, u32[]{:S(2)}) copy-start(f32[128]{0:T(128)} %param.22) | copy-start | bytes 1540
  7.2 39.7 %copy-start.9 = (f32[128]{0:T(128)S(1)}, f32[128]{0:T(128)}, u32[]{:S(2)}) copy-start(f32[128]{0:T(128)} %param.21) | copy-start | bytes 1540
  7.2 150.1 %all-gather.4.cloned.1.call-start = ((), (), s32[]{:S(2)}) async-start(), calls=%async_computation.4 | async-start | bytes 3342336 | tf_op jit(solution)/shard_map/all_gather | solution.py:117
  8.0 153.1 %all-gather.6.cloned.1.call-start = ((), (), s32[]{:S(2)}) async-start(), calls=%async_computation.5 | async-start | bytes 3342336 | tf_op jit(solution)/shard_map/all_gather | solution.py:118
  51.7 2.3 copy-start.4
  51.8 2.3 copy-start.6
  59.7 8.0 %copy-start.11 = (s32[1,16]{1,0:T(1,128)S(1)}, s32[1,16]{1,0:T(1,128)}, u32[]{:S(2)}) copy-start(s32[1,16]{1,0:T(1,128)} %param.32) | copy-start | bytes 196
  59.7 8.1 %copy-start.10 = (s32[2]{0:T(128)S(1)}, s32[2]{0:T(128)}, u32[]{:S(2)}) copy-start(s32[2]{0:T(128)} %constant.75) | copy-start | bytes 28
  62.7 30.3 %all-to-all-start = ((f32[8,64,256]{2,1,0:T(8,128)}), f32[8,64,256]{2,1,0:T(8,128)}, u32[]{:S(2)}, u32[]{:S(2)}) async-start(f32[8,64,256]{2,1,0:T(8,128)} %bitcast.131), calls=%async_computation | async-start | bytes 1048576 | tf_op jit(solution)/shard_map/all_to_all | solution.py:84
  67.0 130.9 %all-gather.8.cloned.1.call-start = ((), (), s32[]{:S(2)}) async-start(), calls=%async_computation.6 | async-start | bytes 3342336 | tf_op jit(solution)/shard_map/all_gather | solution.py:119
  74.5 6.7 %copy-start.12 = (s32[1,16]{1,0:T(1,128)S(1)}, s32[1,16]{1,0:T(1,128)}, u32[]{:S(2)}) copy-start(s32[1,16]{1,0:T(1,128)} %param.33) | copy-start | bytes 196
  93.0 7.0 %copy-start.3 = (bf16[16,512,128]{2,1,0:T(8,128)(2,1)S(1)}, bf16[16,512,128]{2,1,0:T(8,128)(2,1)}, u32[]{:S(2)}) copy-start(bf16[16,512,128]{2,1,0:T(8,128)(2,1)} %get-tuple-element.9) | copy-start | bytes 6291460
  93.0 41.3 %all-to-all-start.2 = ((bf16[16,512,128]{2,1,0:T(8,128)(2,1)}), bf16[16,512,128]{2,1,0:T(8,128)(2,1)}, u32[]{:S(2)}, u32[]{:S(2)}) async-start(bf16[16,512,128]{2,1,0:T(8,128)(2,1)} %gather_fusion.3), calls=%async_computation.2 | async-start | bytes 4194304 | tf_op jit(solution)/shard_map/all_to_all | solution.py:155
  102.2 41.0 %copy-start.5 = (bf16[64,256]{1,0:T(8,128)(2,1)S(1)}, bf16[64,256]{1,0:T(8,128)(2,1)}, u32[]{:S(2)}) copy-start(bf16[64,256]{1,0:T(8,128)(2,1)} %param.19) | copy-start | bytes 98308
  102.2 55.2 %copy-start.7 = (f32[2048]{0:T(1024)S(1)}, f32[2048]{0:T(1024)}, u32[]{:S(2)}) copy-start(f32[2048]{0:T(1024)} %param.34) | copy-start | bytes 24580
  134.3 71.4 %all-to-all-start.3 = ((bf16[16,512,128]{2,1,0:T(8,128)(2,1)}), bf16[16,512,128]{2,1,0:T(8,128)(2,1)S(1)}, u32[]{:S(2)}, u32[]{:S(2)}) async-start(bf16[16,512,128]{2,1,0:T(8,128)(2,1)} %gather_fusion.6), calls=%async_computation.3 | async-start | bytes 4194304 | tf_op jit(solution)/shard_map/all_to_all | solution.py:158
Sparse Core Ops, SparseCore 0:
  10.2 50.2 all-gather.3
  62.7 59.2 all-gather.5
  124.2 73.6 all-gather.7
where the time goes:
time: 234 us; the launch traced here: 233 us
  waiting for transfers between devices  71.1 us (30%)
  blocking collectives  44.7 us (19%)
  local copies, waits for them, and re-layouts  43.6 us (19%)
  matrix products  24.7 us (11%)
  starting transfers between devices  19.2 us (8%)
  other arithmetic  16 us (7%)
  between operations  14.2 us (6%)
    all_gather x1, waiting for transfers between devices, per_device(): down_w = lax.all_gather(w_down, 'req', axis=1, tiled=True)  36.9 us
    all_to_all x1, waiting for transfers between devices, per_device(): lax.all_to_all(place_cache(k_pool, new_keys), 'req', split_axis=0, concat...  32.1 us
    all_gather x1, blocking collectives, per_device(): whole_rows = lax.all_gather(hidden, 'kv', axis=1, tiled=True)  15.6 us
    all_to_all x1, blocking collectives, reduce_to_slice(): arrived = lax.all_to_all(pieces, 'kv', 0, 0, tiled=True)  15.1 us
    all_gather x1, blocking collectives, per_device(): mid_stream = lax.all_gather(mid_slice, 'kv', axis=1, tiled=True)  14 us
    gather x2, local copies, waits for them, and re-layouts, place_cache(): cached = pool[moved_pages].reshape(mig_count, slot_count, channels)  8.49 us
    scatter x1, local copies, waits for them, and re-layouts, attend_pool(): first_pos = jnp.zeros((pool_pages,), jnp.int32).at[targets].set(jnp.tile(...  8.04 us
    scatter x1, local copies, waits for them, and re-layouts, attend_pool(): owner = jnp.full((pool_pages,), -1, jnp.int32).at[targets].set(jnp.repeat...  8.04 us
  transfers between devices with their start and end apart: 6, of which 2 were waited for; matrix products, arithmetic and copies ran while one was open for 33% of the time, Pallas kernels for 0%

commit v1 on v0

--- a/solution.py
+++ b/solution.py
@@ -6,6 +6,12 @@
 MIGP = 4
 EPSILON = 1e-06
 ROPE_BASE = 1000000.0
+
+
+def in_order(tiles, dim):
+    tiles = jnp.moveaxis(tiles, 0, dim)
+    lengths = tiles.shape
+    return tiles.reshape(*lengths[:dim], lengths[dim] * lengths[dim + 1], *lengths[dim + 2 :])
 
 
 def rms_norm(values, scale_row):
@@ -116,7 +122,19 @@
     model_width = mlp_gain.shape[0]
     gate_w = lax.all_gather(w_gate, "req", axis=1, tiled=True)
     up_w = lax.all_gather(w_up, "req", axis=1, tiled=True)
-    down_w = lax.all_gather(w_down, "req", axis=1, tiled=True)
+    size = lax.axis_size("req")
+    pairs = [(i, (i + 1) % size) for i in range(size)]
+    back = [(b, a) for a, b in pairs]
+    lower, upper = ([], [])
+    for step in range(size - 1):
+        if step % 2 == 0:
+            lower.append(lax.ppermute(lower[-1] if lower else w_down, "req", pairs))
+        else:
+            upper.append(lax.ppermute(upper[-1] if upper else w_down, "req", back))
+    blocks = jnp.stack([*lower[::-1], w_down, *upper])
+    shift = lax.axis_index("req") - len(lower)
+    blocks = blocks[(jnp.arange(size) - shift) % size]
+    down_w = in_order(blocks, 1)
     whole_rows = lax.all_gather(hidden, "kv", axis=1, tiled=True)
     normed = rms_norm(whole_rows, attn_gain).astype(jnp.bfloat16)
     query_raw = jnp.dot(normed, w_q, preferred_element_type=jnp.float32).reshape(

time: 234 us -> 268 us (1.15)
  starting transfers between devices: 19.2 us -> 51.7 us
  local copies, waits for them, and re-layouts: 43.6 us -> 68.8 us
  waiting for transfers between devices: 71.1 us -> 46.4 us
  blocking collectives: 44.7 us -> 47.9 us
    ppermute x0 -> x15, waiting for transfers between devices: none -> 37.6 us  [the longest x7 27.7 us: per_device(): upper.append(lax.ppermute(upper[-1] if upper else w_down, 'req', back))]
    all_gather x1 -> x0, waiting for transfers between devices: 36.9 us -> none  [per_device(): down_w = lax.all_gather(w_down, 'req', axis=1, tiled=True)]
    ppermute x0 -> x15, starting transfers between devices: none -> 36.7 us  [the longest x7 34.5 us: per_device(): upper.append(lax.ppermute(upper[-1] if upper else w_down, 'req', back))]
    all_to_all x1, waiting for transfers between devices: 32.1 us -> 0.01 us  [per_device(): lax.all_to_all(place_cache(k_pool, new_keys), 'req', split_axis=0, concat...]
    unnamed x28 -> x60, local copies, waits for them, and re-layouts: 4.5 us -> 26.1 us
    all_to_all x1, waiting for transfers between devices: 0.01 us -> 8.07 us  [per_device(): lax.all_to_all(place_cache(v_pool, new_values), 'req', split_axis=0, conc...]
    all_to_all x1, starting transfers between devices: 7.78 us -> 4.44 us  [per_device(): lax.all_to_all(place_cache(v_pool, new_values), 'req', split_axis=0, conc...]
  transfers between devices with their start and end apart: 6 -> 20, of which waited for: 2 -> 6; matrix products, arithmetic and copies ran while one was open for 33% -> 37% of each run, Pallas kernels for 0% -> 0%
where the time goes in v1:
time: 268 us; the launch traced here: 267 us
  local copies, waits for them, and re-layouts  68.8 us (26%)
  starting transfers between devices  51.7 us (19%)
  blocking collectives  47.9 us (18%)
  waiting for transfers between devices  46.4 us (17%)
  matrix products  23.8 us (9%)
  between operations  14.6 us (5%)
  other arithmetic  13.9 us (5%)
    ppermute x7, starting transfers between devices, per_device(): upper.append(lax.ppermute(upper[-1] if upper else w_down, 'req', back))  34.5 us
    ppermute x7, waiting for transfers between devices, per_device(): upper.append(lax.ppermute(upper[-1] if upper else w_down, 'req', back))  27.7 us
    unnamed x60, local copies, waits for them, and re-layouts  26.1 us
    all_to_all x1, blocking collectives, reduce_to_slice(): arrived = lax.all_to_all(pieces, 'kv', 0, 0, tiled=True)  17.7 us
    all_gather x1, blocking collectives, per_device(): mid_stream = lax.all_gather(mid_slice, 'kv', axis=1, tiled=True)  15.1 us
    all_gather x1, blocking collectives, per_device(): whole_rows = lax.all_gather(hidden, 'kv', axis=1, tiled=True)  15.1 us
    ppermute x8, waiting for transfers between devices, per_device(): lower.append(lax.ppermute(lower[-1] if lower else w_down, 'req', pairs))  9.89 us
    gather x2, local copies, waits for them, and re-layouts, place_cache(): cached = pool[moved_pages].reshape(mig_count, slot_count, channels)  9.58 us
  transfers between devices with their start and end apart: 20, of which 6 were waited for; matrix products, arithmetic and copies ran while one was open for 37% of the time, Pallas kernels for 0%

profile of v1, /device:TPU:1, one launch (start us, length us, event | category | flops | bytes accessed | tf_op | source)
XLA Modules:
  0.0 267.2 jit_solution(13403678380837663358)
XLA Ops:
  13.2 15.1 %all_gather.12 = bf16[64,2048]{1,0:T(8,128)(2,1)S(1)} all-gather(bf16[64,256]{1,0:T(8,128)(2,1)} %param.19), channel_id=1, replica_groups=mesh['req'=16,'kv'=8] {'kv'}, dimensions={1}, use_global_device_ids=true | all-gather | bytes 294912 | tf_op jit(solution)/shard_map/all_gather | solution.py:138
  32.9 8.0 %scatter_custom_fusion.1 = s32[174]{0:T(256)S(1)} fusion(s32[2048]{0:T(1024)S(1)} %bitcast.179, s32[2048]{0:T(1024)S(1)} %reshape.636, s32[]{:T(128)} %constant.39.clone.1), kind=kCustom, calls=%fused_computation.150 | custom fusion | bytes 700 | tf_op jit(solution)/shard_map/scatter | solution.py:55
  41.0 8.2 %scatter_custom_fusion = s32[174]{0:T(256)S(1)} fusion(s32[2048]{0:T(1024)S(1)} %bitcast.180, s32[2048]{0:T(1024)S(1)} %reshape.628, s32[]{:T(128)} %constant.34.clone.1), kind=kCustom, calls=%fused_computation.153 | custom fusion | bytes 700 | tf_op jit(solution)/shard_map/scatter | solution.py:50
  51.6 4.3 %fusion.82 = (f32[64,2]{0,1:T(2,128)S(1)}, f32[64,1,2,22272]{3,0,2,1:T(8,128)S(1)}) fusion(bf16[64,2,128]{2,0,1:T(8,128)(2,1)S(1)} %pad_maximum_fusion, bf16[22272,128,1]{1,0,2:T(8,128)(2,1)} %bitcast.173, pred[64,22272]{1,0:T(8,128)(4,1)S(1)} %fusion.5), kind=kOutput, calls=%fused_computation.167 | convolution fusion | flops 738361216 | bytes 18563584 | tf_op jit(solution)/shard_map/rkgd,tkd->rkgt/dot_general | solution.py:65
  58.6 5.2 %fusion.20 = f32[64,1,2,128]{3,0,2,1:T(8,128)S(1)} fusion(bf16[22272,128,1]{1,0,2:T(8,128)(2,1)} %bitcast.177, f32[64,2]{0,1:T(2,128)S(1)} %get-tuple-element.12, f32[64,1,2,22272]{3,0,2,1:T(8,128)S(1)} %get-tuple-element.26, f32[64,2]{0,1:T(2,128)S(1)} %fusion.59, f32[64,128]{1,0:T(8,128)S(1)} %get-tuple-element.27, f32[64,2]{0,1:T(2,128)S(1)} %get-tuple-element.11), kind=kOutput, calls=%fused_computation.39 | convolution fusion | flops 738394112 | bytes 17204736 | tf_op jit(solution)/shard_map/rkgt,tkd->rkgd/dot_general | solution.py:82
  66.8 4.3 %all-to-all-start = ((f32[8,64,256]{2,1,0:T(8,128)}), f32[8,64,256]{2,1,0:T(8,128)S(1)}, u32[]{:S(2)}, u32[]{:S(2)}) async-start(f32[8,64,256]{2,1,0:T(8,128)} %bitcast.169), calls=%async_computation | async-start | bytes 1048576 | tf_op jit(solution)/shard_map/all_to_all | solution.py:90
  74.9 4.8 %gather_fusion.5 = bf16[64,128,128]{2,1,0:T(8,128)(2,1)} fusion(bf16[174,128,128]{2,1,0:T(8,128)(2,1)} %param.29, s32[1024]{0:T(1024)S(1)} %get-tuple-element.29), kind=kCustom, calls=%fused_computation.5 | custom fusion | bytes 4194560 | tf_op jit(solution)/shard_map/gather | solution.py:165
  79.7 4.8 %gather_fusion.2 = bf16[64,128,128]{2,1,0:T(8,128)(2,1)} fusion(bf16[174,128,128]{2,1,0:T(8,128)(2,1)} %param.28, s32[1024]{0:T(1024)S(1)} %get-tuple-element.29), kind=kCustom, calls=%fused_computation.2 | custom fusion | bytes 4194560 | tf_op jit(solution)/shard_map/gather | solution.py:165
  86.5 7.3 %bitcast_select_fusion = (bf16[16,512,128]{2,1,0:T(8,128)(2,1)S(1)}, bf16[16,512,128]{2,1,0:T(8,128)(2,1)}) fusion(pred[16,512]{1,0:T(8,128)(4,1)S(1)} %get-tuple-element.18, pred[16,512]{1,0:T(8,128)(4,1)S(1)} %get-tuple-element.17, bf16[16,128]{1,0:T(8,128)(2,1)S(1)} %gather_fusion.6, bf16[16,128]{1,0:T(8,128)(2,1)S(1)} %gather_fusion.3, ...), kind=kLoop, calls=%fused_computation.27 | loop fusion | flops 4194304 | bytes 8413184 | tf_op jit(solution)/shard_map/jit(_where)/select_n | solution.py:167
  97.9 4.8 %collective-permute-start.9 = (bf16[2048,48]{0,1:T(8,128)(2,1)S(1)}, bf16[2048,48]{0,1:T(8,128)(2,1)S(1)}, u32[]{:S(2)}, u32[]{:S(2)}) collective-permute-start(bf16[2048,48]{0,1:T(8,128)(2,1)S(1)} %collective-permute-done.8), channel_id=1, source_target_pairs={{8,0},{16,8},{24,16},{32,24},{40,32},{48,40},{56,48},{64,56},{72,6... | collective-permute-start | bytes 589832 | tf_op jit(solution)/shard_map/ppermute | solution.py:133
  112.2 4.8 %collective-permute-start.10 = (bf16[2048,48]{0,1:T(8,128)(2,1)S(1)}, bf16[2048,48]{0,1:T(8,128)(2,1)}, u32[]{:S(2)}, u32[]{:S(2)}) collective-permute-start(bf16[2048,48]{0,1:T(8,128)(2,1)S(1)} %collective-permute-done.9), channel_id=1, source_target_pairs={{8,0},{16,8},{24,16},{32,24},{40,32},{48,40},{56,48},{64,56},{72,6... | collective-permute-start | bytes 589832 | tf_op jit(solution)/shard_map/ppermute | solution.py:133
  120.0 6.2 %all-to-all-start.2 = ((bf16[16,512,128]{2,1,0:T(8,128)(2,1)}), bf16[16,512,128]{2,1,0:T(8,128)(2,1)S(1)}, u32[]{:S(2)}, u32[]{:S(2)}) async-start(bf16[16,512,128]{2,1,0:T(8,128)(2,1)} %gather_fusion.4), calls=%async_computation.2 | async-start | bytes 4194304 | tf_op jit(solution)/shard_map/all_to_all | solution.py:173
  126.3 4.8 %collective-permute-start.11 = (bf16[2048,48]{0,1:T(8,128)(2,1)}, bf16[2048,48]{0,1:T(8,128)(2,1)S(1)}, u32[]{:S(2)}, u32[]{:S(2)}) collective-permute-start(bf16[2048,48]{0,1:T(8,128)(2,1)} %collective-permute-done.10), channel_id=1, source_target_pairs={{8,0},{16,8},{24,16},{32,24},{40,32},{48,40},{56,48},{64,56},{72,6... | collective-permute-start | bytes 589832 | tf_op jit(solution)/shard_map/ppermute | solution.py:133
  131.1 23.6 %collective-permute-done.11 = bf16[2048,48]{0,1:T(8,128)(2,1)S(1)} collective-permute-done((bf16[2048,48]{0,1:T(8,128)(2,1)}, bf16[2048,48]{0,1:T(8,128)(2,1)S(1)}, u32[]{:S(2)}, u32[]{:S(2)}) %collective-permute-start.11) | collective-permute-done | bytes 196640 | tf_op jit(solution)/shard_map/ppermute | solution.py:133
  154.7 5.6 %collective-permute-start.12 = (bf16[2048,48]{0,1:T(8,128)(2,1)S(1)}, bf16[2048,48]{0,1:T(8,128)(2,1)S(1)}, u32[]{:S(2)}, u32[]{:S(2)}) collective-permute-start(bf16[2048,48]{0,1:T(8,128)(2,1)S(1)} %collective-permute-done.11), channel_id=1, source_target_pairs={{8,0},{16,8},{24,16},{32,24},{40,32},{48,40},{56,48},{64,56},{72,6... | collective-permute-start | bytes 589832 | tf_op jit(solution)/shard_map/ppermute | solution.py:133
  160.3 15.1 %all_gather.13 = bf16[64,2048]{1,0:T(8,128)(2,1)S(1)} all-gather(bf16[64,256]{1,0:T(8,128)(2,1)S(1)} %add_convert_fusion.1), channel_id=1, replica_groups=mesh['req'=16,'kv'=8] {'kv'}, dimensions={1}, use_global_device_ids=true | all-gather | bytes 294912 | tf_op jit(solution)/shard_map/all_gather | solution.py:190
  175.6 5.1 %collective-permute-start.13 = (bf16[2048,48]{0,1:T(8,128)(2,1)S(1)}, bf16[2048,48]{0,1:T(8,128)(2,1)}, u32[]{:S(2)}, u32[]{:S(2)}) collective-permute-start(bf16[2048,48]{0,1:T(8,128)(2,1)S(1)} %collective-permute-done.12), channel_id=1, source_target_pairs={{8,0},{16,8},{24,16},{32,24},{40,32},{48,40},{56,48},{64,56},{72,6... | collective-permute-start | bytes 589832 | tf_op jit(solution)/shard_map/ppermute | solution.py:133
  180.7 4.1 %collective-permute-done.13 = bf16[2048,48]{0,1:T(8,128)(2,1)} collective-permute-done((bf16[2048,48]{0,1:T(8,128)(2,1)S(1)}, bf16[2048,48]{0,1:T(8,128)(2,1)}, u32[]{:S(2)}, u32[]{:S(2)}) %collective-permute-start.13) | collective-permute-done | bytes 196640 | tf_op jit(solution)/shard_map/ppermute | solution.py:133
  184.8 5.6 %collective-permute-start.14 = (bf16[2048,48]{0,1:T(8,128)(2,1)}, bf16[2048,48]{0,1:T(8,128)(2,1)}, u32[]{:S(2)}, u32[]{:S(2)}) collective-permute-start(bf16[2048,48]{0,1:T(8,128)(2,1)} %collective-permute-done.13), channel_id=1, source_target_pairs={{8,0},{16,8},{24,16},{32,24},{40,32},{48,40},{56,48},{64,56},{72,6... | collective-permute-start | bytes 589832 | tf_op jit(solution)/shard_map/ppermute | solution.py:133
  205.0 4.4 %all-to-all-start.3 = ((bf16[16,512,128]{2,1,0:T(8,128)(2,1)}), bf16[16,512,128]{2,1,0:T(8,128)(2,1)}, u32[]{:S(2)}, u32[]{:S(2)}) async-start(bf16[16,512,128]{2,1,0:T(8,128)(2,1)} %gather_fusion.7), calls=%async_computation.3 | async-start | bytes 4194304 | tf_op jit(solution)/shard_map/all_to_all | solution.py:176
  218.9 3.8 %fusion.39 = f32[64,768]{1,0:T(8,128)} fusion(bf16[2048,768]{0,1:T(8,128)(2,1)} %all-gather.3.cloned.1.call-done, bf16[64,2048]{1,0:T(8,128)(2,1)S(1)} %all_gather.13, f32[2048]{0:T(1024)S(1)} %copy-done.15, f32[64]{0:T(128)S(1)} %add_rsqrt_fusion.1), kind=kOutput, calls=%fused_computation.77 | convolution fusion | flops 201850880 | bytes 3612928 | tf_op jit(solution)/shard_map/dot_general | solution.py:192
  222.7 4.9 %fusion.8 = f32[8,64,256]{2,1,0:T(8,128)} fusion(bf16[8,256,768]{1,0,2:T(8,128)(2,1)S(1)} %bitcast.172, bf16[2048,768]{0,1:T(8,128)(2,1)} %all-gather.5.cloned.1.call-done, f32[64,768]{1,0:T(8,128)} %fusion.39, bf16[64,2048]{1,0:T(8,128)(2,1)S(1)} %all_gather.13, f32[2048]{0:T(1024)S(1)} %copy-done.15, f32[64]{0:T(128)S(1)} %add_rsqrt_fusion.1), kind=kOutput, calls=%fused_computation.29 | convolution fusion | flops 403472384 | bytes 7282944 | tf_op jit(solution)/shard_map/ru,cu->rc/dot_general | solution.py:195
  227.6 8.1 %all-to-all-done.3 = bf16[16,512,128]{2,1,0:T(8,128)(2,1)} async-done(((bf16[16,512,128]{2,1,0:T(8,128)(2,1)}), bf16[16,512,128]{2,1,0:T(8,128)(2,1)}, u32[]{:S(2)}, u32[]{:S(2)}) %all-to-all-start.3) | async-done | bytes 2097184 | tf_op jit(solution)/shard_map/all_to_all | solution.py:176
  235.6 17.7 %all_to_all.20 = f32[8,64,256]{2,1,0:T(8,128)S(1)} all-to-all(f32[8,64,256]{2,1,0:T(8,128)} %fusion.8), channel_id=1, replica_groups=mesh['req'=16,'kv'=8] {'kv'}, dimensions={0} | all-to-all | bytes 1048576 | tf_op jit(solution)/shard_map/all_to_all | solution.py:90
  (165 shorter events, 71.9 us)
Async XLA Ops:
  7.2 56.7 %copy-start = (bf16[256,2048]{1,0:T(8,128)(2,1)S(1)}, bf16[256,2048]{1,0:T(8,128)(2,1)}, u32[]{:S(2)}) copy-start(bf16[256,2048]{1,0:T(8,128)(2,1)} %param.27) | copy-start | bytes 3145732
  7.2 43.9 %copy-start.17 = (f32[128]{0:T(128)S(1)}, f32[128]{0:T(128)}, u32[]{:S(2)}) copy-start(f32[128]{0:T(128)} %param.21) | copy-start | bytes 1540
  7.2 211.6 %all-gather.3.cloned.1.call-start = ((), (), s32[]{:S(2)}) async-start(), calls=%async_computation.4 | async-start | bytes 3342336 | tf_op jit(solution)/shard_map/all_gather | solution.py:123
  7.3 79.2 %collective-permute-start = (bf16[2048,48]{0,1:T(8,128)(2,1)}, bf16[2048,48]{0,1:T(8,128)(2,1)S(1)}, u32[]{:S(2)}, u32[]{:S(2)}) collective-permute-start(bf16[2048,48]{0,1:T(8,128)(2,1)} %param.37), channel_id=1, source_target_pairs={{0,8},{8,16},{16,24},{24,32},{32,40},{40,48},{48,56},{56,64},{64,7... | collective-permute-start | bytes 589832 | tf_op jit(solution)/shard_map/ppermute | solution.py:131
  9.5 88.5 %collective-permute-start.8 = (bf16[2048,48]{0,1:T(8,128)(2,1)}, bf16[2048,48]{0,1:T(8,128)(2,1)S(1)}, u32[]{:S(2)}, u32[]{:S(2)}) collective-permute-start(bf16[2048,48]{0,1:T(8,128)(2,1)} %param.37), channel_id=1, source_target_pairs={{8,0},{16,8},{24,16},{32,24},{40,32},{48,40},{56,48},{64,56},{72,6... | collective-permute-start | bytes 589832 | tf_op jit(solution)/shard_map/ppermute | solution.py:133
  66.8 53.2 %all-to-all-start = ((f32[8,64,256]{2,1,0:T(8,128)}), f32[8,64,256]{2,1,0:T(8,128)S(1)}, u32[]{:S(2)}, u32[]{:S(2)}) async-start(f32[8,64,256]{2,1,0:T(8,128)} %bitcast.169), calls=%async_computation | async-start | bytes 1048576 | tf_op jit(solution)/shard_map/all_to_all | solution.py:90
  71.1 151.6 %all-gather.5.cloned.1.call-start = ((), (), s32[]{:S(2)}) async-start(), calls=%async_computation.5 | async-start | bytes 3342336 | tf_op jit(solution)/shard_map/all_gather | solution.py:124
  86.4 10.8 %collective-permute-start.1 = (bf16[2048,48]{0,1:T(8,128)(2,1)S(1)}, bf16[2048,48]{0,1:T(8,128)(2,1)S(1)}, u32[]{:S(2)}, u32[]{:S(2)}) collective-permute-start(bf16[2048,48]{0,1:T(8,128)(2,1)S(1)} %collective-permute-done), channel_id=1, source_target_pairs={{0,8},{8,16},{16,24},{24,32},{32,40},{40,48},{48,56},{56,64},{64,7... | collective-permute-start | bytes 589832 | tf_op jit(solution)/shard_map/ppermute | solution.py:131
  97.2 8.9 %collective-permute-start.2 = (bf16[2048,48]{0,1:T(8,128)(2,1)S(1)}, bf16[2048,48]{0,1:T(8,128)(2,1)S(1)}, u32[]{:S(2)}, u32[]{:S(2)}) collective-permute-start(bf16[2048,48]{0,1:T(8,128)(2,1)S(1)} %collective-permute-done.1), channel_id=1, source_target_pairs={{0,8},{8,16},{16,24},{24,32},{32,40},{40,48},{48,56},{56,64},{64,7... | collective-permute-start | bytes 589832 | tf_op jit(solution)/shard_map/ppermute | solution.py:131
  97.9 14.2 %collective-permute-start.9 = (bf16[2048,48]{0,1:T(8,128)(2,1)S(1)}, bf16[2048,48]{0,1:T(8,128)(2,1)S(1)}, u32[]{:S(2)}, u32[]{:S(2)}) collective-permute-start(bf16[2048,48]{0,1:T(8,128)(2,1)S(1)} %collective-permute-done.8), channel_id=1, source_target_pairs={{8,0},{16,8},{24,16},{32,24},{40,32},{48,40},{56,48},{64,56},{72,6... | collective-permute-start | bytes 589832 | tf_op jit(solution)/shard_map/ppermute | solution.py:133
  106.2 13.8 %collective-permute-start.3 = (bf16[2048,48]{0,1:T(8,128)(2,1)S(1)}, bf16[2048,48]{0,1:T(8,128)(2,1)}, u32[]{:S(2)}, u32[]{:S(2)}) collective-permute-start(bf16[2048,48]{0,1:T(8,128)(2,1)S(1)} %collective-permute-done.2), channel_id=1, source_target_pairs={{0,8},{8,16},{16,24},{24,32},{32,40},{40,48},{48,56},{56,64},{64,7... | collective-permute-start | bytes 589832 | tf_op jit(solution)/shard_map/ppermute | solution.py:131
  112.2 48.2 %copy-start.10 = (bf16[2048,48]{0,1:T(8,128)(2,1)}, bf16[2048,48]{0,1:T(8,128)(2,1)S(1)}, u32[]{:S(2)}) copy-start(bf16[2048,48]{0,1:T(8,128)(2,1)S(1)} %collective-permute-done.9) | copy-start | bytes 589828
  112.2 14.1 %collective-permute-start.10 = (bf16[2048,48]{0,1:T(8,128)(2,1)S(1)}, bf16[2048,48]{0,1:T(8,128)(2,1)}, u32[]{:S(2)}, u32[]{:S(2)}) collective-permute-start(bf16[2048,48]{0,1:T(8,128)(2,1)S(1)} %collective-permute-done.9), channel_id=1, source_target_pairs={{8,0},{16,8},{24,16},{32,24},{40,32},{48,40},{56,48},{64,56},{72,6... | collective-permute-start | bytes 589832 | tf_op jit(solution)/shard_map/ppermute | solution.py:133
  120.0 11.0 %collective-permute-start.4 = (bf16[2048,48]{0,1:T(8,128)(2,1)}, bf16[2048,48]{0,1:T(8,128)(2,1)}, u32[]{:S(2)}, u32[]{:S(2)}) collective-permute-start(bf16[2048,48]{0,1:T(8,128)(2,1)} %collective-permute-done.3), channel_id=1, source_target_pairs={{0,8},{8,16},{16,24},{24,32},{32,40},{40,48},{48,56},{56,64},{64,7... | collective-permute-start | bytes 589832 | tf_op jit(solution)/shard_map/ppermute | solution.py:131
  120.0 85.0 %all-to-all-start.2 = ((bf16[16,512,128]{2,1,0:T(8,128)(2,1)}), bf16[16,512,128]{2,1,0:T(8,128)(2,1)S(1)}, u32[]{:S(2)}, u32[]{:S(2)}) async-start(bf16[16,512,128]{2,1,0:T(8,128)(2,1)} %gather_fusion.4), calls=%async_computation.2 | async-start | bytes 4194304 | tf_op jit(solution)/shard_map/all_to_all | solution.py:173
  126.2 74.4 %copy-start.7 = (bf16[2048,48]{0,1:T(8,128)(2,1)S(1)}, bf16[2048,48]{0,1:T(8,128)(2,1)}, u32[]{:S(2)}) copy-start(bf16[2048,48]{0,1:T(8,128)(2,1)} %param.37) | copy-start | bytes 589828
  126.3 28.4 %collective-permute-start.11 = (bf16[2048,48]{0,1:T(8,128)(2,1)}, bf16[2048,48]{0,1:T(8,128)(2,1)S(1)}, u32[]{:S(2)}, u32[]{:S(2)}) collective-permute-start(bf16[2048,48]{0,1:T(8,128)(2,1)} %collective-permute-done.10), channel_id=1, source_target_pairs={{8,0},{16,8},{24,16},{32,24},{40,32},{48,40},{56,48},{64,56},{72,6... | collective-permute-start | bytes 589832 | tf_op jit(solution)/shard_map/ppermute | solution.py:133
  131.0 29.3 %collective-permute-start.5 = (bf16[2048,48]{0,1:T(8,128)(2,1)}, bf16[2048,48]{0,1:T(8,128)(2,1)S(1)}, u32[]{:S(2)}, u32[]{:S(2)}) collective-permute-start(bf16[2048,48]{0,1:T(8,128)(2,1)} %collective-permute-done.4), channel_id=1, source_target_pairs={{0,8},{8,16},{16,24},{24,32},{32,40},{40,48},{48,56},{56,64},{64,7... | collective-permute-start | bytes 589832 | tf_op jit(solution)/shard_map/ppermute | solution.py:131
  154.7 20.9 %collective-permute-start.12 = (bf16[2048,48]{0,1:T(8,128)(2,1)S(1)}, bf16[2048,48]{0,1:T(8,128)(2,1)S(1)}, u32[]{:S(2)}, u32[]{:S(2)}) collective-permute-start(bf16[2048,48]{0,1:T(8,128)(2,1)S(1)} %collective-permute-done.11), channel_id=1, source_target_pairs={{8,0},{16,8},{24,16},{32,24},{40,32},{48,40},{56,48},{64,56},{72,6... | collective-permute-start | bytes 589832 | tf_op jit(solution)/shard_map/ppermute | solution.py:133
  160.3 20.4 %collective-permute-start.6 = (bf16[2048,48]{0,1:T(8,128)(2,1)S(1)}, bf16[2048,48]{0,1:T(8,128)(2,1)S(1)}, u32[]{:S(2)}, u32[]{:S(2)}) collective-permute-start(bf16[2048,48]{0,1:T(8,128)(2,1)S(1)} %collective-permute-done.5), channel_id=1, source_target_pairs={{0,8},{8,16},{16,24},{24,32},{32,40},{40,48},{48,56},{56,64},{64,7... | collective-permute-start | bytes 589832 | tf_op jit(solution)/shard_map/ppermute | solution.py:131
  175.6 9.2 %collective-permute-start.13 = (bf16[2048,48]{0,1:T(8,128)(2,1)S(1)}, bf16[2048,48]{0,1:T(8,128)(2,1)}, u32[]{:S(2)}, u32[]{:S(2)}) collective-permute-start(bf16[2048,48]{0,1:T(8,128)(2,1)S(1)} %collective-permute-done.12), channel_id=1, source_target_pairs={{8,0},{16,8},{24,16},{32,24},{40,32},{48,40},{56,48},{64,56},{72,6... | collective-permute-start | bytes 589832 | tf_op jit(solution)/shard_map/ppermute | solution.py:133
  180.7 9.7 %collective-permute-start.7 = (bf16[2048,48]{0,1:T(8,128)(2,1)S(1)}, bf16[2048,48]{0,1:T(8,128)(2,1)S(1)}, u32[]{:S(2)}, u32[]{:S(2)}) collective-permute-start(bf16[2048,48]{0,1:T(8,128)(2,1)S(1)} %collective-permute-done.6), channel_id=1, source_target_pairs={{0,8},{8,16},{16,24},{24,32},{32,40},{40,48},{48,56},{56,64},{64,7... | collective-permute-start | bytes 589832 | tf_op jit(solution)/shard_map/ppermute | solution.py:131
  184.8 27.0 %collective-permute-start.14 = (bf16[2048,48]{0,1:T(8,128)(2,1)}, bf16[2048,48]{0,1:T(8,128)(2,1)}, u32[]{:S(2)}, u32[]{:S(2)}) collective-permute-start(bf16[2048,48]{0,1:T(8,128)(2,1)} %collective-permute-done.13), channel_id=1, source_target_pairs={{8,0},{16,8},{24,16},{32,24},{40,32},{48,40},{56,48},{64,56},{72,6... | collective-permute-start | bytes 589832 | tf_op jit(solution)/shard_map/ppermute | solution.py:133
  205.0 30.6 %all-to-all-start.3 = ((bf16[16,512,128]{2,1,0:T(8,128)(2,1)}), bf16[16,512,128]{2,1,0:T(8,128)(2,1)}, u32[]{:S(2)}, u32[]{:S(2)}) async-start(bf16[16,512,128]{2,1,0:T(8,128)(2,1)} %gather_fusion.7), calls=%async_computation.3 | async-start | bytes 4194304 | tf_op jit(solution)/shard_map/all_to_all | solution.py:176
  (17 other events, 250.9 us)
Sparse Core Ops, SparseCore 0:
  13.3 47.1 all-gather.2
  74.1 50.4 all-gather.4
